TPU v7x, 128 devices: a whole 4x4x4 slice. The times are simulated.
128 devices in a mesh: section: 4 (over x), sample: 8 (over z, y_lo), tensor: 4 (over y_hi, core).
Axes of the slice: x: 4, y: 4 (y_hi: 2, y_lo: 2; y = y_hi * 2 + y_lo), z: 4, core: 2. Of those that a mesh axis runs over, the one named last changes fastest.
Arguments:
- queries: bfloat16 [4, 1024, 8192], P('section', 'sample', 'tensor'), may hold values from -4.5 to 4.5
- suffix_keys: bfloat16 [4, 1024, 1024], P('section', 'sample', 'tensor'), may hold values from -4.5 to 4.5
- suffix_values: bfloat16 [4, 1024, 1024], P('section', 'sample', 'tensor'), may hold values from -4.5 to 4.5
- output_grad: bfloat16 [4, 1024, 8192], P('section', 'sample', 'tensor'), may hold values from -192 to 192
- prefix_keys: bfloat16 [4, 4096, 1024], P('section', ('sample', 'tensor')), may hold values from -4.5 to 4.5
- prefix_values: bfloat16 [4, 4096, 1024], P('section', ('sample', 'tensor')), may hold values from -4.5 to 4.5
- kv_weight: bfloat16 [4, 8192, 2, 1024], P('section', None, None, 'tensor'), may hold values from -0.0625 to 0.0625
- prefix_states: bfloat16 [4, 4096, 8192], P('section', ('sample', 'tensor')), may hold values from -6 to 6
- norm_gain: bfloat16 [4, 8192], P('section'), may hold values from 0.099609375 to 1.8984375
- segment_ids: int32 [8, 128], P('sample'), may hold values from 0 to 1, never falling along the last dimension, each value on 1 to 96 neighbouring positions
- segment_prompt: int32 [8, 2], P('sample'), may hold values from 0 to 2
- block_table: int32 [3, 16], replicated, may hold values from 0 to 31, as said below
Outputs:
- query_grad: bfloat16 [4, 1024, 8192], P('section', 'sample', 'tensor')
- rollout_key_gradient: bfloat16 [4, 1024, 1024], P('section', 'sample', 'tensor')
- suffix_value_grad: bfloat16 [4, 1024, 1024], P('section', 'sample', 'tensor')
- prefix_key_grad: float32 [4, 4096, 1024], P('section', ('sample', 'tensor'))
- prefix_value_grad: float32 [4, 4096, 1024], P('section', ('sample', 'tensor'))
- prefix_state_gradient: float32 [4, 4096, 8192], P('section', ('sample', 'tensor'))
Inputs may be any that keep to these rules, and one draw needn't show every extreme that they name: `block_table`: each row lists 16 distinct pages; its first 8 entries are the same pages in every row, and every page of the pool appears in some row.
All inputs are finite; a program needn't handle non-finite values.
Results may differ from a plain program's by a relative error of at most 0.024.
Values may be sent and summed in bfloat16 or wider, within the bound.
No kernel may reach another device: no remote copies, remote signals or barrier semaphores. Data moves between devices by JAX's collectives and lax.ppermute only.
A program may use at most 192 MiB of HBM per device.

v0:
```python
import jax
import jax.numpy as jnp
from jax import lax
from jax.sharding import PartitionSpec as P

HEAD_SIZE = 128
PAGE = 128
MASKED_SCORE = -1e30
EPSILON = 1e-05


def entering(value, axis, join, neutral):
    count = lax.axis_size(axis)
    place = lax.axis_index(axis)
    ahead = count - 1 - place
    gathered = lax.all_gather(value.astype(jnp.bfloat16), axis)
    state = jnp.zeros_like(value) + jnp.asarray(neutral, value.dtype)

    def one(turn, state):
        source = count - 1 - turn
        return join(state, lax.dynamic_index_in_dim(gathered, source, 0, False).astype(value.dtype))

    return lax.fori_loop(0, ahead, one, state)


def visible_keys(seg_row, prompt_row, table, pooled_rows):
    tok_count = seg_row.shape[0]
    seg_hot = seg_row[:, None] == jnp.arange(prompt_row.shape[0], dtype=jnp.int32)[None, :]
    prompt_tok = jnp.sum(jnp.where(seg_hot, prompt_row[None, :], 0), axis=1)
    page_ids = jnp.arange(pooled_rows // PAGE, dtype=jnp.int32)
    member = jnp.any(table[:, :, None] == page_ids[None, None, :], axis=1)
    prompt_hot = prompt_tok[:, None] == jnp.arange(table.shape[0], dtype=jnp.int32)[None, :]
    member_tok = jnp.any(prompt_hot[:, :, None] & member[None, :, :], axis=1)
    prefix_seen = jnp.repeat(member_tok, PAGE, axis=1)
    position = jnp.arange(tok_count, dtype=jnp.int32)
    suffix_seen = (seg_row[:, None] == seg_row[None, :]) & (position[None, :] <= position[:, None])
    return jnp.concatenate([prefix_seen, suffix_seen], axis=1)


def attend_group(query_grp, grad_grp, key_rows, value_rows, visible):
    inv_root = query_grp.shape[-1] ** (-0.5)
    scores = (
        jnp.einsum("rgd,kd->rgk", query_grp, key_rows, preferred_element_type=jnp.float32)
        * inv_root
    )
    scores = jnp.where(visible[:, None, :], scores, MASKED_SCORE)
    row_max = jnp.max(scores, axis=2, keepdims=True)
    exponent = jnp.exp(scores - row_max)
    softmax_w = exponent / jnp.sum(exponent, axis=2, keepdims=True)
    weights_low = softmax_w.astype(jnp.bfloat16)
    attended = jnp.einsum(
        "rgk,kd->rgd", weights_low, value_rows, preferred_element_type=jnp.float32
    )
    delta_row = jnp.sum(grad_grp.astype(jnp.float32) * attended, axis=2, keepdims=True)
    weight_grad = jnp.einsum(
        "rgd,kd->rgk", grad_grp, value_rows, preferred_element_type=jnp.float32
    )
    score_grad = (softmax_w * (weight_grad - delta_row)).astype(jnp.bfloat16)
    query_out = (
        jnp.einsum("rgk,kd->rgd", score_grad, key_rows, preferred_element_type=jnp.float32)
        * inv_root
    )
    key_result = (
        jnp.einsum("rgk,rgd->kd", score_grad, query_grp, preferred_element_type=jnp.float32)
        * inv_root
    )
    value_out = jnp.einsum("rgk,rgd->kd", weights_low, grad_grp, preferred_element_type=jnp.float32)
    return (query_out, key_result, value_out)


def add_terms(earlier, later_term):
    return earlier + later_term


def on_device(
    queries,
    suffix_keys,
    suffix_values,
    output_grad,
    prefix_keys,
    prefix_values,
    kv_weight,
    prefix_states,
    norm_gain,
    segment_ids,
    segment_prompt,
    block_table,
):
    head_width = suffix_keys.shape[2]
    key_store, value_store = (
        lax.all_gather(prefix_keys, ("sample", "tensor"), axis=1, tiled=True),
        lax.all_gather(prefix_values, ("sample", "tensor"), axis=1, tiled=True),
    )
    offset = lax.axis_index("tensor") * head_width
    key_pool = lax.dynamic_slice_in_dim(key_store, offset, head_width, 2)[0]
    value_pool = lax.dynamic_slice_in_dim(value_store, offset, head_width, 2)[0]
    pooled_rows = key_pool.shape[0]
    tok_count = queries.shape[1]
    kv_local = head_width // HEAD_SIZE
    group_size = queries.shape[2] // head_width
    visible = visible_keys(segment_ids[0], segment_prompt[0], block_table, pooled_rows)
    query_rows = queries[0].reshape(tok_count, kv_local, group_size, HEAD_SIZE)
    grad_rows = output_grad[0].reshape(tok_count, kv_local, group_size, HEAD_SIZE)
    own_keys = suffix_keys[0]
    own_values = suffix_values[0]
    query_pieces, suffix_key_pieces, suffix_value_pieces, prefix_key_pieces, prefix_value_pieces = (
        [],
        [],
        [],
        [],
        [],
    )
    for head_index in range(kv_local):
        low_col = head_index * HEAD_SIZE
        key_rows = jnp.concatenate(
            [
                key_pool[:, low_col : low_col + HEAD_SIZE],
                own_keys[:, low_col : low_col + HEAD_SIZE],
            ],
            axis=0,
        )
        value_rows = jnp.concatenate(
            [
                value_pool[:, low_col : low_col + HEAD_SIZE],
                own_values[:, low_col : low_col + HEAD_SIZE],
            ],
            axis=0,
        )
        query_out, key_result, value_out = attend_group(
            query_rows[:, head_index], grad_rows[:, head_index], key_rows, value_rows, visible
        )
        query_pieces.append(query_out)
        prefix_key_pieces.append(key_result[:pooled_rows])
        suffix_key_pieces.append(key_result[pooled_rows:])
        prefix_value_pieces.append(value_out[:pooled_rows])
        suffix_value_pieces.append(value_out[pooled_rows:])
    query_grad = jnp.stack(query_pieces, axis=1).reshape(tok_count, -1).astype(jnp.bfloat16)
    rollout_key_gradient = jnp.concatenate(suffix_key_pieces, axis=1).astype(jnp.bfloat16)
    suffix_value_grad = jnp.concatenate(suffix_value_pieces, axis=1).astype(jnp.bfloat16)
    pooled_key = jnp.concatenate(prefix_key_pieces, axis=1)
    pooled_value = jnp.concatenate(prefix_value_pieces, axis=1)
    key_reduced, value_reduced = (
        lax.psum_scatter(
            pooled_key.astype(jnp.bfloat16), "sample", scatter_dimension=0, tiled=True
        ).astype(jnp.float32),
        lax.psum_scatter(
            pooled_value.astype(jnp.bfloat16), "sample", scatter_dimension=0, tiled=True
        ).astype(jnp.float32),
    )
    key_home, value_home = (
        lax.all_to_all(
            key_reduced.astype(jnp.bfloat16), "tensor", split_axis=0, concat_axis=1, tiled=True
        ).astype(key_reduced.dtype),
        lax.all_to_all(
            value_reduced.astype(jnp.bfloat16), "tensor", split_axis=0, concat_axis=1, tiled=True
        ).astype(value_reduced.dtype),
    )
    stacked = jnp.stack(
        [key_reduced.astype(jnp.bfloat16), value_reduced.astype(jnp.bfloat16)], axis=1
    )
    weight_local = kv_weight[0]
    normed_grad = lax.psum_scatter(
        lax.dot_general(
            stacked, weight_local, (((1, 2), (1, 2)), ((), ())), preferred_element_type=jnp.float32
        ).astype(jnp.bfloat16),
        "tensor",
        scatter_dimension=0,
        tiled=True,
    ).astype(jnp.float32)
    states = prefix_states[0].astype(jnp.float32)
    gain_wide = norm_gain[0].astype(jnp.float32)[None, :]
    inv_rms = lax.rsqrt(jnp.mean(states * states, axis=1, keepdims=True) + EPSILON)
    gained = gain_wide * normed_grad
    layer_term = inv_rms * gained - states * inv_rms**3 * jnp.mean(
        states * gained, axis=1, keepdims=True
    )
    higher_terms = entering(layer_term, "section", add_terms, jnp.zeros_like(layer_term))
    prefix_state_gradient = higher_terms + layer_term
    return (
        query_grad[None],
        rollout_key_gradient[None],
        suffix_value_grad[None],
        key_home[None],
        value_home[None],
        prefix_state_gradient[None],
    )


def solution(mesh):
    placed = (
        P("section", "sample", "tensor"),
        P("section", "sample", "tensor"),
        P("section", "sample", "tensor"),
        P("section", "sample", "tensor"),
        P("section", ("sample", "tensor"), None),
        P("section", ("sample", "tensor"), None),
        P("section", None, None, "tensor"),
        P("section", ("sample", "tensor"), None),
        P("section", None),
        P("sample", None),
        P("sample", None),
        P(),
    )
    return jax.shard_map(
        on_device,
        mesh=mesh,
        in_specs=placed,
        out_specs=(
            P("section", "sample", "tensor"),
            P("section", "sample", "tensor"),
            P("section", "sample", "tensor"),
            P("section", ("sample", "tensor"), None),
            P("section", ("sample", "tensor"), None),
            P("section", ("sample", "tensor"), None),
        ),
        check_vma=False,
    )
```

profile of v0, /device:TPU:1, one launch (start us, length us, event | category | flops | bytes accessed | tf_op | source)
XLA Modules:
  0.0 552.3 jit_solution(3952926247144493262)
XLA Ops:
  8.8 2.0 copy.107
  10.8 1.3 copy.109
  13.8 65.7 %all-gather.5.cloned.1.call-done = bf16[1,4096,1024]{2,1,0:T(8,128)(2,1)} async-done(((bf16[1,128,1024]{2,1,0:T(8,128)(2,1)}), bf16[1,4096,1024]{2,1,0:T(8,128)(2,1)}) %all-gather.5.cloned.1.call-update) | async-done | bytes 8388624 | tf_op jit(solution)/shard_map/all_gather | solution.py:91
  79.6 67.3 %all-gather.7.cloned.1.call-done = bf16[1,4096,1024]{2,1,0:T(8,128)(2,1)} async-done(((bf16[1,128,1024]{2,1,0:T(8,128)(2,1)}), bf16[1,4096,1024]{2,1,0:T(8,128)(2,1)}) %all-gather.7.cloned.1.call-update) | async-done | bytes 8388624 | tf_op jit(solution)/shard_map/all_gather | solution.py:92
  146.8 2.5 dynamic-slice_bitcast_fusion
  149.4 1.5 fusion.61
  152.0 2.4 fusion.33
  154.4 10.7 %fusion.67 = (f32[128,8]{0,1:T(8,128)S(1)}, f32[128,8,4224]{0,2,1:T(8,128)}) fusion(f32[4224,128,8]{1,0,2:T(8,128)S(1)} %fusion.33, pred[128,4224]{0,1:T(8,128)(4,1)S(1)} %pad_add_fusion), kind=kOutput, calls=%fused_computation.118 | output fusion | flops 17305728 | bytes 35147776 | tf_op jit(solution)/shard_map/sub | solution.py:48
  165.1 7.5 %fusion.13 = bf16[128,8,4224]{0,2,1:T(8,128)(2,1)S(1)} fusion(f32[128,8,4224]{0,2,1:T(8,128)} %get-tuple-element.112, f32[128,8]{0,1:T(8,128)S(1)} %get-tuple-element.111), kind=kLoop, calls=%fused_computation.23 | loop fusion | flops 8650752 | bytes 25956352 | tf_op jit(solution)/shard_map/convert_element_type | solution.py:50
  172.6 4.4 copy-done.2
  176.9 2.5 fusion.28
  179.6 7.1 %fusion.3 = bf16[128,8,4224]{0,2,1:T(8,128)(2,1)} fusion(f32[128,8]{0,1:T(8,128)S(1)} %fusion.28, f32[128,8,4224]{0,2,1:T(8,128)S(1)} %bitcast.161, f32[128,8]{0,1:T(8,128)S(1)} %get-tuple-element.111, bf16[128,128]{1,0:T(8,128)(2,1)S(1)} %get-tuple-element.103, bf16[4096,128]{1,0:T(8,128)(2,1)} %get-tuple-element.97, bf16[128,2,8,128]{0,3,2,1:T(8,128)(2,1)} %bitcast.168), kind=kOutput, calls=%fused_computation.7 | convolution fusion | flops 1126760448 | bytes 27303936 | tf_op jit(solution)/shard_map/rgd,kd->rgk/dot_general | solution.py:55
  186.8 6.4 %fusion.17 = bf16[4224,128]{0,1:T(8,128)(2,1)S(1)} fusion(bf16[128,8,4224]{0,2,1:T(8,128)(2,1)} %fusion.3, bf16[128,2,8,128]{0,3,2,1:T(8,128)(2,1)} %bitcast.163), kind=kOutput, calls=%fused_computation.34 | convolution fusion | flops 1108377600 | bytes 9994240 | tf_op jit(solution)/shard_map/rgk,rgd->kd/dot_general | solution.py:64
  194.1 2.4 fusion.32
  196.5 10.2 %fusion.66 = (f32[128,8]{0,1:T(8,128)S(1)}, f32[128,8,4224]{0,2,1:T(8,128)}) fusion(f32[4224,128,8]{1,0,2:T(8,128)S(1)} %fusion.32, pred[128,4224]{0,1:T(8,128)(4,1)S(1)} %pad_add_fusion), kind=kOutput, calls=%fused_computation.117 | output fusion | flops 17305728 | bytes 35147776 | tf_op jit(solution)/shard_map/sub | solution.py:48
  206.8 7.5 %fusion.14 = bf16[128,8,4224]{0,2,1:T(8,128)(2,1)S(1)} fusion(f32[128,8,4224]{0,2,1:T(8,128)} %get-tuple-element.110, f32[128,8]{0,1:T(8,128)S(1)} %get-tuple-element.109), kind=kLoop, calls=%fused_computation.24 | loop fusion | flops 8650752 | bytes 25956352 | tf_op jit(solution)/shard_map/convert_element_type | solution.py:50
  214.3 4.4 copy-done.3
  218.6 2.5 fusion.29
  221.3 7.2 %fusion.2 = bf16[128,8,4224]{0,2,1:T(8,128)(2,1)} fusion(f32[128,8]{0,1:T(8,128)S(1)} %fusion.29, f32[128,8,4224]{0,2,1:T(8,128)S(1)} %bitcast.159, f32[128,8]{0,1:T(8,128)S(1)} %get-tuple-element.109, bf16[128,128]{1,0:T(8,128)(2,1)S(1)} %get-tuple-element.104, bf16[4096,128]{1,0:T(8,128)(2,1)} %get-tuple-element.98, bf16[128,2,8,128]{0,3,2,1:T(8,128)(2,1)} %bitcast.169), kind=kOutput, calls=%fused_computation.4 | convolution fusion | flops 1126760448 | bytes 27303936 | tf_op jit(solution)/shard_map/rgd,kd->rgk/dot_general | solution.py:55
  228.5 6.4 %fusion.18 = bf16[4224,128]{0,1:T(8,128)(2,1)S(1)} fusion(bf16[128,8,4224]{0,2,1:T(8,128)(2,1)} %fusion.2, bf16[128,2,8,128]{0,3,2,1:T(8,128)(2,1)S(1)} %bitcast.166), kind=kOutput, calls=%fused_computation.35 | convolution fusion | flops 1108377600 | bytes 9994240 | tf_op jit(solution)/shard_map/rgk,rgd->kd/dot_general | solution.py:64
  236.0 1.5 pad_maximum_fusion
  237.6 6.3 %fusion.19 = bf16[4224,128]{0,1:T(8,128)(2,1)S(1)} fusion(bf16[128,8,4224]{0,2,1:T(8,128)(2,1)} %copy-done.2, bf16[128,2,8,128]{0,3,2,1:T(8,128)(2,1)S(1)} %bitcast.170), kind=kOutput, calls=%fused_computation.36 | convolution fusion | flops 1107836928 | bytes 9994240 | tf_op jit(solution)/shard_map/rgk,rgd->kd/dot_general | solution.py:67
  244.0 1.0 copy-done.13
  245.1 6.4 %fusion.20 = bf16[4224,128]{0,1:T(8,128)(2,1)S(1)} fusion(bf16[128,8,4224]{0,2,1:T(8,128)(2,1)} %copy-done.3, bf16[128,2,8,128]{0,3,2,1:T(8,128)(2,1)S(1)} %bitcast.171), kind=kOutput, calls=%fused_computation.37 | convolution fusion | flops 1107836928 | bytes 9994240 | tf_op jit(solution)/shard_map/rgk,rgd->kd/dot_general | solution.py:67
  251.6 1.6 pad_maximum_fusion.1
  253.5 35.6 %reduce-scatter.4.cloned.1.call-done = bf16[512,256]{0,1:T(8,128)(2,1)} async-done(((bf16[4096,256]{0,1:T(8,128)(2,1)}), bf16[512,256]{0,1:T(8,128)(2,1)}) %reduce-scatter.4.cloned.1.call-update) | async-done | bytes 262160 | tf_op jit(solution)/shard_map/reduce_scatter | solution.py:143
  289.1 54.1 %reduce-scatter.6.cloned.1.call-done = bf16[512,256]{0,1:T(8,128)(2,1)} async-done(((bf16[4096,256]{0,1:T(8,128)(2,1)}), bf16[512,256]{0,1:T(8,128)(2,1)}) %reduce-scatter.6.cloned.1.call-update) | async-done | bytes 262160 | tf_op jit(solution)/shard_map/reduce_scatter | solution.py:146
  343.2 11.4 %bitcast_convert_fusion = bf16[512,8192]{1,0:T(8,128)(2,1)} fusion(bf16[8192,2,256]{2,1,0:T(2,128)(2,1)} %bitcast.185, bf16[512,1,256]{0,2,1:T(8,128)(2,1)} %bitcast.180, bf16[512,1,256]{0,2,1:T(8,128)(2,1)} %bitcast.179), kind=kOutput, calls=%fused_computation.11 | convolution fusion | flops 4299423744 | bytes 17301504 | tf_op jit(solution)/shard_map/dot_general | solution.py:163
  355.5 76.9 %reduce-scatter.8.cloned.1.call-done = bf16[128,8192]{1,0:T(8,128)(2,1)} async-done(((bf16[512,8192]{1,0:T(8,128)(2,1)}), bf16[128,8192]{1,0:T(8,128)(2,1)}) %reduce-scatter.8.cloned.1.call-update) | async-done | bytes 2097168 | tf_op jit(solution)/shard_map/reduce_scatter | solution.py:162
  432.4 2.8 fusion.21
  435.2 2.8 fusion.25
  438.1 5.1 fusion.31
  443.2 5.0 fusion.30
  448.3 1.0 copy.135
  452.4 1.7 copy_bitcast_fusion
  454.1 4.4 all-to-all-start.1
  459.2 5.8 %all-to-all-done.1 = bf16[4,128,256]{1,2,0:T(8,128)(2,1)S(1)} async-done(((bf16[4,128,256]{1,2,0:T(8,128)(2,1)}), bf16[4,128,256]{1,2,0:T(8,128)(2,1)S(1)}, u32[]{:S(2)}, u32[]{:S(2)}) %all-to-all-start.1) | async-done | bytes 262176 | tf_op jit(solution)/shard_map/all_to_all | solution.py:154
  465.0 4.3 all-to-all-start
  470.9 1.0 copy.139
  471.9 4.0 all-to-all-done
  475.9 1.0 copy.138
  476.9 43.8 %all-gather.9.cloned.1.call-done = bf16[512,8192]{1,0:T(8,128)(2,1)} async-done(((bf16[128,8192]{1,0:T(8,128)(2,1)}), bf16[512,8192]{1,0:T(8,128)(2,1)}) %all-gather.9.cloned.1.call-update) | async-done | bytes 8388624 | tf_op jit(solution)/shard_map/all_gather | solution.py:16
  520.7 2.5 broadcast_in_dim.42
  523.1 15.9 %while.12 = (s32[]{:T(128)}, f32[128,8192]{1,0:T(8,128)}, s32[]{:T(128)}, bf16[4,128,8192]{2,1,0:T(8,128)(2,1)}, s32[]{:T(128)}, /*index=5*/s32[]{:T(128)}, s32[]{:T(128)}, s32[]{:T(128)}) while((s32[]{:T(128)}, f32[128,8192]{1,0:T(8,128)}, s32[]{:T(128)}, bf16[4,128,8192]{2,1,0:T(8,128)(2,1)}, s32[]{:T(128)}, /*index=5*/s32[]{:T(128)}, ...), condition=%wide.region_15.16_spmd, body=%wide.region_14.15_spmd.sunk | while | flops 2097158 | bytes 10485903 | solution.py:23
  523.1 5.3 convert_add_fusion.2
  528.4 5.3 convert_add_fusion.2
  533.7 5.3 convert_add_fusion.2
  539.0 6.1 %add_bitcast_fusion = f32[1,128,8192]{2,1,0:T(8,128)} fusion(f32[128,8192]{1,0:T(8,128)} %get-tuple-element.62, bf16[128,8192]{1,0:T(8,128)(2,1)} %reduce-scatter.8.cloned.1.call-done, bf16[1,128,8192]{2,1,0:T(8,128)(2,1)S(1)} %copy-done, f32[128]{0:T(128)S(1)} %broadcast_multiply_fusion, f32[128]{0:T(128)S(1)} %get-tuple-element.108, ...), kind=kLoop, calls=%fused_computation.42 | loop fusion | flops 8388608 | bytes 12617216 | tf_op jit(solution)/shard_map/broadcast_in_dim | solution.py:185
  (116 shorter events, 13.4 us)
Async XLA Ops:
  7.2 6.0 %copy-start.25 = (s32[1,2]{1,0:T(1,128)S(1)}, s32[1,2]{1,0:T(1,128)}, u32[]{:S(2)}) copy-start(s32[1,2]{1,0:T(1,128)} %param.24) | copy-start | bytes 28
  7.2 6.0 %copy-start.23 = (s32[1,128]{1,0:T(1,128)S(1)}, s32[1,128]{1,0:T(1,128)}, u32[]{:S(2)}) copy-start(s32[1,128]{1,0:T(1,128)} %param.23) | copy-start | bytes 1540
  7.2 6.1 %copy-start.24 = (s32[3,16]{1,0:T(4,128)S(1)}, s32[3,16]{1,0:T(4,128)}, u32[]{:S(2)}) copy-start(s32[3,16]{1,0:T(4,128)} %param.25) | copy-start | bytes 580
  7.2 6.4 %copy-start.20 = (bf16[1,128,256]{2,1,0:T(8,128)(2,1)S(1)}, bf16[1,128,256]{2,1,0:T(8,128)(2,1)}, u32[]{:S(2)}) copy-start(bf16[1,128,256]{2,1,0:T(8,128)(2,1)} %param.15) | copy-start | bytes 196612
  7.2 6.4 %copy-start.21 = (bf16[1,128,256]{2,1,0:T(8,128)(2,1)S(1)}, bf16[1,128,256]{2,1,0:T(8,128)(2,1)}, u32[]{:S(2)}) copy-start(bf16[1,128,256]{2,1,0:T(8,128)(2,1)} %param.16) | copy-start | bytes 196612
  7.2 72.3 %all-gather.5.cloned.1.call-start = ((), (), s32[]{:S(2)}) async-start(), calls=%async_computation.5 | async-start | bytes 8650752 | tf_op jit(solution)/shard_map/all_gather | solution.py:91
  8.0 138.9 %all-gather.7.cloned.1.call-start = ((), (), s32[]{:S(2)}) async-start(), calls=%async_computation.6 | async-start | bytes 8650752 | tf_op jit(solution)/shard_map/all_gather | solution.py:92
  8.7 280.4 %reduce-scatter.4.cloned.1.call-start = ((), (), s32[]{:S(2)}) async-start(), calls=%async_computation.7 | async-start | bytes 2359296 | tf_op jit(solution)/shard_map/reduce_scatter | solution.py:143
  12.1 137.2 %copy-start.9 = (bf16[1,128,2048]{1,2,0:T(8,128)(2,1)}, bf16[1,128,2048]{1,2,0:T(8,128)(2,1)S(1)}, u32[]{:S(2)}) copy-start(bf16[1,128,2048]{1,2,0:T(8,128)(2,1)S(1)} %copy.109) | copy-start | bytes 1572868
  13.6 137.4 %copy-start.18 = (bf16[128,128]{1,0:T(8,128)(2,1)}, bf16[128,128]{1,0:T(8,128)(2,1)S(1)}, u32[]{:S(2)}) copy-start(bf16[128,128]{1,0:T(8,128)(2,1)S(1)} %get-tuple-element.105) | copy-start | bytes 98308
  149.4 2.6 copy-start.6
  151.0 1.0 copy-start.4
  165.0 11.9 %copy-start.15 = (bf16[4096,128]{1,0:T(8,128)(2,1)S(1)}, bf16[4096,128]{1,0:T(8,128)(2,1)}, u32[]{:S(2)}) copy-start(bf16[4096,128]{1,0:T(8,128)(2,1)} %get-tuple-element.97) | copy-start | bytes 3145732
  165.0 11.9 %copy-start.17 = (bf16[128,1,8,128]{3,0,2,1:T(8,128)(2,1)S(1)}, bf16[128,1,8,128]{3,0,2,1:T(8,128)(2,1)}, u32[]{:S(2)}) copy-start(bf16[128,1,8,128]{3,0,2,1:T(8,128)(2,1)} %copy.164) | copy-start | bytes 786436
  165.0 14.4 %slice-start.5 = ((s8[17301504]{0:T(1024)(128)(4,1)}), s8[4194304]{0:T(1024)(128)(4,1)S(1)}, s32[]{:S(2)}) async-start(s8[17301504]{0:T(1024)(128)(4,1)} %bitcast.160), calls=%async_computation.16 | async-start | bytes 8388608
  165.0 14.4 %slice-start.6 = ((s8[17301504]{0:T(1024)(128)(4,1)}), s8[4194304]{0:T(1024)(128)(4,1)S(1)}, s32[]{:S(2)}) async-start(s8[17301504]{0:T(1024)(128)(4,1)} %bitcast.160), calls=%async_computation.17 | async-start | bytes 8388608
  165.0 14.4 %slice-start.7 = ((s8[17301504]{0:T(1024)(128)(4,1)}), s8[4194304]{0:T(1024)(128)(4,1)S(1)}, s32[]{:S(2)}) async-start(s8[17301504]{0:T(1024)(128)(4,1)} %bitcast.160), calls=%async_computation.18 | async-start | bytes 8388608
  165.1 14.4 %slice-start.8 = ((s8[17301504]{0:T(1024)(128)(4,1)}), s8[4194304]{0:T(1024)(128)(4,1)S(1)}, s32[]{:S(2)}) async-start(s8[17301504]{0:T(1024)(128)(4,1)} %bitcast.160), calls=%async_computation.19 | async-start | bytes 8388608
  172.5 4.4 copy-start.2
  176.9 2.7 slice-start.9
  186.7 7.4 %copy-start.7 = (bf16[1,128,2048]{1,2,0:T(8,128)(2,1)S(1)}, bf16[1,128,2048]{1,2,0:T(8,128)(2,1)}, u32[]{:S(2)}) copy-start(bf16[1,128,2048]{1,2,0:T(8,128)(2,1)} %copy.107) | copy-start | bytes 1572868
  193.2 1.0 copy-start.5
  206.7 11.9 %copy-start.14 = (bf16[4096,128]{1,0:T(8,128)(2,1)S(1)}, bf16[4096,128]{1,0:T(8,128)(2,1)}, u32[]{:S(2)}) copy-start(bf16[4096,128]{1,0:T(8,128)(2,1)} %get-tuple-element.98) | copy-start | bytes 3145732
  206.7 14.4 %slice-start = ((s8[17301504]{0:T(1024)(128)(4,1)}), s8[4194304]{0:T(1024)(128)(4,1)S(1)}, s32[]{:S(2)}) async-start(s8[17301504]{0:T(1024)(128)(4,1)} %bitcast.158), calls=%async_computation.11 | async-start | bytes 8388608
  206.7 14.4 %slice-start.1 = ((s8[17301504]{0:T(1024)(128)(4,1)}), s8[4194304]{0:T(1024)(128)(4,1)S(1)}, s32[]{:S(2)}) async-start(s8[17301504]{0:T(1024)(128)(4,1)} %bitcast.158), calls=%async_computation.12 | async-start | bytes 8388608
  206.7 14.4 %slice-start.2 = ((s8[17301504]{0:T(1024)(128)(4,1)}), s8[4194304]{0:T(1024)(128)(4,1)S(1)}, s32[]{:S(2)}) async-start(s8[17301504]{0:T(1024)(128)(4,1)} %bitcast.158), calls=%async_computation.13 | async-start | bytes 8388608
  206.7 14.4 %slice-start.3 = ((s8[17301504]{0:T(1024)(128)(4,1)}), s8[4194304]{0:T(1024)(128)(4,1)S(1)}, s32[]{:S(2)}) async-start(s8[17301504]{0:T(1024)(128)(4,1)} %bitcast.158), calls=%async_computation.14 | async-start | bytes 8388608
  214.2 4.4 copy-start.3
  218.6 2.6 slice-start.4
  221.3 7.2 %copy-start.8 = (bf16[1,128,2048]{1,2,0:T(8,128)(2,1)S(1)}, bf16[1,128,2048]{1,2,0:T(8,128)(2,1)}, u32[]{:S(2)}) copy-start(bf16[1,128,2048]{1,2,0:T(8,128)(2,1)} %copy.107) | copy-start | bytes 1572868
  228.5 7.5 %slice-start.10 = ((bf16[4224,128]{0,1:T(8,128)(2,1)}), bf16[4096,128]{0,1:T(8,128)(2,1)S(1)}, s32[]{:S(2)}) async-start(bf16[4224,128]{0,1:T(8,128)(2,1)} %copy-done.5), calls=%async_computation.21 | async-start | bytes 2097152 | tf_op jit(solution)/shard_map/slice | solution.py:133
  234.9 1.0 copy-start.11
  235.9 1.7 copy-start.10
  237.6 105.6 %reduce-scatter.6.cloned.1.call-start = ((), (), s32[]{:S(2)}) async-start(), calls=%async_computation.8 | async-start | bytes 2359296 | tf_op jit(solution)/shard_map/reduce_scatter | solution.py:146
  244.0 1.0 copy-start.13
  251.5 1.7 copy-start.12
  253.2 179.2 %reduce-scatter.8.cloned.1.call-start = ((), (), s32[]{:S(2)}) async-start(), calls=%async_computation.9 | async-start | bytes 10485760 | tf_op jit(solution)/shard_map/reduce_scatter | solution.py:162
  354.7 0.8 copy-start.22
  354.7 77.7 %copy-start = (bf16[1,128,8192]{2,1,0:T(8,128)(2,1)S(1)}, bf16[1,128,8192]{2,1,0:T(8,128)(2,1)}, u32[]{:S(2)}) copy-start(bf16[1,128,8192]{2,1,0:T(8,128)(2,1)} %param.21) | copy-start | bytes 6291460
  354.7 166.0 %all-gather.9.cloned.1.call-start = ((), (), s32[]{:S(2)}) async-start(), calls=%async_computation.10 | async-start | bytes 10485760 | tf_op jit(solution)/shard_map/all_gather | solution.py:16
  432.4 2.8 copy-start.1
  435.2 2.9 copy-start.19
  443.2 15.2 %copy-start.16 = (bf16[512,256]{0,1:T(8,128)(2,1)S(1)}, bf16[512,256]{0,1:T(8,128)(2,1)}, u32[]{:S(2)}) copy-start(bf16[512,256]{0,1:T(8,128)(2,1)} %reduce-scatter.4.cloned.1.call-done) | copy-start | bytes 786436
  454.1 10.9 %all-to-all-start.1 = ((bf16[4,128,256]{1,2,0:T(8,128)(2,1)}), bf16[4,128,256]{1,2,0:T(8,128)(2,1)S(1)}, u32[]{:S(2)}, u32[]{:S(2)}) async-start(bf16[4,128,256]{1,2,0:T(8,128)(2,1)} %copy_bitcast_fusion), calls=%async_computation.3 | async-start | bytes 524288 | tf_op jit(solution)/shard_map/all_to_all | solution.py:154
  465.0 10.9 %all-to-all-start = ((bf16[4,128,256]{1,2,0:T(8,128)(2,1)}), bf16[4,128,256]{1,2,0:T(8,128)(2,1)S(1)}, u32[]{:S(2)}, u32[]{:S(2)}) async-start(bf16[4,128,256]{1,2,0:T(8,128)(2,1)} %copy_bitcast_fusion.1), calls=%async_computation.1 | async-start | bytes 524288 | tf_op jit(solution)/shard_map/all_to_all | solution.py:151
Sparse Core Ops, SparseCore 0:
  9.7 69.7 all-gather.4
  81.3 65.5 all-gather.6
  237.7 51.3 reduce-scatter.3
  291.4 51.8 reduce-scatter.5
  354.8 77.5 reduce-scatter.7
  438.2 82.4 all-gather.8
where the time goes:
time: 557 us; the launch traced here: 552 us
  waiting for transfers between devices  355 us (64%)
  matrix products  71.2 us (13%)
  other arithmetic  67.1 us (12%)
  local copies, waits for them, and re-layouts  35.1 us (6%)
  between operations  14.9 us (3%)
  starting transfers between devices  9.21 us (2%)
    reduce_scatter x1, waiting for transfers between devices, on_device(): lax.psum_scatter(lax.dot_general(stacked, weight_local, (((1, 2), (1, 2))...  76.9 us
    all_gather x1, waiting for transfers between devices, on_device(): lax.all_gather(prefix_values, ('sample', 'tensor'), axis=1, tiled=True)  67.3 us
    all_gather x1, waiting for transfers between devices, on_device(): lax.all_gather(prefix_keys, ('sample', 'tensor'), axis=1, tiled=True)  65.7 us
    reduce_scatter x1, waiting for transfers between devices, on_device(): lax.psum_scatter(pooled_value.astype(jnp.bfloat16), 'sample', scatter_dim...  54.1 us
    all_gather x1, waiting for transfers between devices, entering(): gathered = lax.all_gather(value.astype(jnp.bfloat16), axis)  43.8 us
    reduce_scatter x1, waiting for transfers between devices, on_device(): lax.psum_scatter(pooled_key.astype(jnp.bfloat16), 'sample', scatter_dimen...  35.6 us
    unnamed x81, local copies, waits for them, and re-layouts  22.6 us
    sub x2, other arithmetic, attend_group(): exponent = jnp.exp(scores - row_max)  20.9 us
  transfers between devices with their start and end apart: 8, of which 8 were waited for; matrix products, arithmetic and copies ran while one was open for 7% of the time, Pallas kernels for 0%

commit v1 on v0

--- a/solution.py
+++ b/solution.py
@@ -151,8 +151,16 @@
         lax.all_to_all(
             key_reduced.astype(jnp.bfloat16), "tensor", split_axis=0, concat_axis=1, tiled=True
         ).astype(key_reduced.dtype),
-        lax.all_to_all(
-            value_reduced.astype(jnp.bfloat16), "tensor", split_axis=0, concat_axis=1, tiled=True
+        jnp.concatenate(
+            lax.all_to_all(
+                jnp.stack(
+                    jnp.split(value_reduced.astype(jnp.bfloat16), lax.axis_size("tensor"), axis=0)
+                ),
+                "tensor",
+                0,
+                0,
+            ),
+            axis=1,
         ).astype(value_reduced.dtype),
     )
     stacked = jnp.stack(

time: 557 us -> 557 us (level)
  no operation moved by 1% of the time
where the time goes in v1:
time: 557 us; the launch traced here: 552 us
  waiting for transfers between devices  355 us (64%)
  matrix products  71.3 us (13%)
  other arithmetic  67.9 us (12%)
  local copies, waits for them, and re-layouts  34.4 us (6%)
  between operations  14.9 us (3%)
  starting transfers between devices  9.2 us (2%)
    reduce_scatter x1, waiting for transfers between devices, on_device(): lax.psum_scatter(lax.dot_general(stacked, weight_local, (((1, 2), (1, 2))...  76.9 us
    all_gather x1, waiting for transfers between devices, on_device(): lax.all_gather(prefix_values, ('sample', 'tensor'), axis=1, tiled=True)  67.3 us
    all_gather x1, waiting for transfers between devices, on_device(): lax.all_gather(prefix_keys, ('sample', 'tensor'), axis=1, tiled=True)  65.7 us
    reduce_scatter x1, waiting for transfers between devices, on_device(): lax.psum_scatter(pooled_value.astype(jnp.bfloat16), 'sample', scatter_dim...  54.1 us
    all_gather x1, waiting for transfers between devices, entering(): gathered = lax.all_gather(value.astype(jnp.bfloat16), axis)  44.7 us
    reduce_scatter x1, waiting for transfers between devices, on_device(): lax.psum_scatter(pooled_key.astype(jnp.bfloat16), 'sample', scatter_dimen...  35.5 us
    unnamed x81, local copies, waits for them, and re-layouts  22.6 us
    sub x2, other arithmetic, attend_group(): exponent = jnp.exp(scores - row_max)  20.8 us
  transfers between devices with their start and end apart: 8, of which 8 were waited for; matrix products, arithmetic and copies ran while one was open for 7% of the time, Pallas kernels for 0%

profile of v1, /device:TPU:1, one launch (start us, length us, event | category | flops | bytes accessed | tf_op | source)
XLA Modules:
  0.0 552.2 jit_solution(18222744860983658698)
XLA Ops:
  8.8 2.0 copy.106
  10.8 1.3 copy.108
  13.8 65.7 %all-gather.5.cloned.1.call-done = bf16[1,4096,1024]{2,1,0:T(8,128)(2,1)} async-done(((bf16[1,128,1024]{2,1,0:T(8,128)(2,1)}), bf16[1,4096,1024]{2,1,0:T(8,128)(2,1)}) %all-gather.5.cloned.1.call-update) | async-done | bytes 8388624 | tf_op jit(solution)/shard_map/all_gather | solution.py:91
  79.6 67.3 %all-gather.7.cloned.1.call-done = bf16[1,4096,1024]{2,1,0:T(8,128)(2,1)} async-done(((bf16[1,128,1024]{2,1,0:T(8,128)(2,1)}), bf16[1,4096,1024]{2,1,0:T(8,128)(2,1)}) %all-gather.7.cloned.1.call-update) | async-done | bytes 8388624 | tf_op jit(solution)/shard_map/all_gather | solution.py:92
  146.8 2.5 dynamic-slice_bitcast_fusion
  149.4 1.5 fusion.61
  152.0 2.4 fusion.33
  154.4 10.7 %fusion.67 = (f32[128,8]{0,1:T(8,128)S(1)}, f32[128,8,4224]{0,2,1:T(8,128)}) fusion(f32[4224,128,8]{1,0,2:T(8,128)S(1)} %fusion.33, pred[128,4224]{0,1:T(8,128)(4,1)S(1)} %pad_add_fusion), kind=kOutput, calls=%fused_computation.122 | output fusion | flops 17305728 | bytes 35147776 | tf_op jit(solution)/shard_map/sub | solution.py:48
  165.0 7.5 %fusion.13 = bf16[128,8,4224]{0,2,1:T(8,128)(2,1)S(1)} fusion(f32[128,8,4224]{0,2,1:T(8,128)} %get-tuple-element.116, f32[128,8]{0,1:T(8,128)S(1)} %get-tuple-element.115), kind=kLoop, calls=%fused_computation.23 | loop fusion | flops 8650752 | bytes 25956352 | tf_op jit(solution)/shard_map/convert_element_type | solution.py:50
  172.5 4.4 copy-done.2
  176.9 2.5 fusion.28
  179.6 7.1 %fusion.3 = bf16[128,8,4224]{0,2,1:T(8,128)(2,1)} fusion(f32[128,8]{0,1:T(8,128)S(1)} %fusion.28, f32[128,8,4224]{0,2,1:T(8,128)S(1)} %bitcast.164, f32[128,8]{0,1:T(8,128)S(1)} %get-tuple-element.115, bf16[128,128]{1,0:T(8,128)(2,1)S(1)} %get-tuple-element.107, bf16[4096,128]{1,0:T(8,128)(2,1)} %get-tuple-element.97, bf16[128,2,8,128]{0,3,2,1:T(8,128)(2,1)} %bitcast.171), kind=kOutput, calls=%fused_computation.7 | convolution fusion | flops 1126760448 | bytes 27303936 | tf_op jit(solution)/shard_map/rgd,kd->rgk/dot_general | solution.py:55
  186.7 6.4 %fusion.17 = bf16[4224,128]{0,1:T(8,128)(2,1)S(1)} fusion(bf16[128,8,4224]{0,2,1:T(8,128)(2,1)} %fusion.3, bf16[128,2,8,128]{0,3,2,1:T(8,128)(2,1)} %bitcast.166), kind=kOutput, calls=%fused_computation.34 | convolution fusion | flops 1108377600 | bytes 9994240 | tf_op jit(solution)/shard_map/rgk,rgd->kd/dot_general | solution.py:64
  194.1 2.4 fusion.32
  196.5 10.2 %fusion.66 = (f32[128,8]{0,1:T(8,128)S(1)}, f32[128,8,4224]{0,2,1:T(8,128)}) fusion(f32[4224,128,8]{1,0,2:T(8,128)S(1)} %fusion.32, pred[128,4224]{0,1:T(8,128)(4,1)S(1)} %pad_add_fusion), kind=kOutput, calls=%fused_computation.121 | output fusion | flops 17305728 | bytes 35147776 | tf_op jit(solution)/shard_map/sub | solution.py:48
  206.7 7.5 %fusion.14 = bf16[128,8,4224]{0,2,1:T(8,128)(2,1)S(1)} fusion(f32[128,8,4224]{0,2,1:T(8,128)} %get-tuple-element.114, f32[128,8]{0,1:T(8,128)S(1)} %get-tuple-element.113), kind=kLoop, calls=%fused_computation.24 | loop fusion | flops 8650752 | bytes 25956352 | tf_op jit(solution)/shard_map/convert_element_type | solution.py:50
  214.2 4.4 copy-done.3
  218.6 2.5 fusion.29
  221.2 7.2 %fusion.2 = bf16[128,8,4224]{0,2,1:T(8,128)(2,1)} fusion(f32[128,8]{0,1:T(8,128)S(1)} %fusion.29, f32[128,8,4224]{0,2,1:T(8,128)S(1)} %bitcast.162, f32[128,8]{0,1:T(8,128)S(1)} %get-tuple-element.113, bf16[128,128]{1,0:T(8,128)(2,1)S(1)} %get-tuple-element.108, bf16[4096,128]{1,0:T(8,128)(2,1)} %get-tuple-element.98, bf16[128,2,8,128]{0,3,2,1:T(8,128)(2,1)} %bitcast.172), kind=kOutput, calls=%fused_computation.4 | convolution fusion | flops 1126760448 | bytes 27303936 | tf_op jit(solution)/shard_map/rgd,kd->rgk/dot_general | solution.py:55
  228.4 6.4 %fusion.18 = bf16[4224,128]{0,1:T(8,128)(2,1)S(1)} fusion(bf16[128,8,4224]{0,2,1:T(8,128)(2,1)} %fusion.2, bf16[128,2,8,128]{0,3,2,1:T(8,128)(2,1)S(1)} %bitcast.169), kind=kOutput, calls=%fused_computation.35 | convolution fusion | flops 1108377600 | bytes 9994240 | tf_op jit(solution)/shard_map/rgk,rgd->kd/dot_general | solution.py:64
  234.9 1.0 copy-done.11
  236.0 1.5 pad_maximum_fusion
  237.6 6.3 %fusion.19 = bf16[4224,128]{0,1:T(8,128)(2,1)S(1)} fusion(bf16[128,8,4224]{0,2,1:T(8,128)(2,1)} %copy-done.2, bf16[128,2,8,128]{0,3,2,1:T(8,128)(2,1)S(1)} %bitcast.173), kind=kOutput, calls=%fused_computation.36 | convolution fusion | flops 1107836928 | bytes 9994240 | tf_op jit(solution)/shard_map/rgk,rgd->kd/dot_general | solution.py:67
  244.0 1.0 copy-done.13
  245.1 6.4 %fusion.20 = bf16[4224,128]{0,1:T(8,128)(2,1)S(1)} fusion(bf16[128,8,4224]{0,2,1:T(8,128)(2,1)} %copy-done.3, bf16[128,2,8,128]{0,3,2,1:T(8,128)(2,1)S(1)} %bitcast.174), kind=kOutput, calls=%fused_computation.37 | convolution fusion | flops 1107836928 | bytes 9994240 | tf_op jit(solution)/shard_map/rgk,rgd->kd/dot_general | solution.py:67
  251.6 1.6 pad_maximum_fusion.1
  253.5 35.5 %reduce-scatter.4.cloned.1.call-done = bf16[512,256]{0,1:T(8,128)(2,1)} async-done(((bf16[4096,256]{0,1:T(8,128)(2,1)}), bf16[512,256]{0,1:T(8,128)(2,1)}) %reduce-scatter.4.cloned.1.call-update) | async-done | bytes 262160 | tf_op jit(solution)/shard_map/reduce_scatter | solution.py:143
  289.1 54.1 %reduce-scatter.6.cloned.1.call-done = bf16[512,256]{0,1:T(8,128)(2,1)} async-done(((bf16[4096,256]{0,1:T(8,128)(2,1)}), bf16[512,256]{0,1:T(8,128)(2,1)}) %reduce-scatter.6.cloned.1.call-update) | async-done | bytes 262160 | tf_op jit(solution)/shard_map/reduce_scatter | solution.py:146
  343.2 11.5 %bitcast_convert_fusion = bf16[512,8192]{1,0:T(8,128)(2,1)} fusion(bf16[8192,2,256]{2,1,0:T(2,128)(2,1)} %bitcast.188, bf16[512,1,256]{0,2,1:T(8,128)(2,1)} %bitcast.183, bf16[512,1,256]{0,2,1:T(8,128)(2,1)} %bitcast.182), kind=kOutput, calls=%fused_computation.11 | convolution fusion | flops 4299423744 | bytes 17301504 | tf_op jit(solution)/shard_map/dot_general | solution.py:171
  355.4 76.9 %reduce-scatter.8.cloned.1.call-done = bf16[128,8192]{1,0:T(8,128)(2,1)} async-done(((bf16[512,8192]{1,0:T(8,128)(2,1)}), bf16[128,8192]{1,0:T(8,128)(2,1)}) %reduce-scatter.8.cloned.1.call-update) | async-done | bytes 2097168 | tf_op jit(solution)/shard_map/reduce_scatter | solution.py:170
  432.4 2.8 fusion.21
  435.2 2.8 fusion.25
  438.1 5.1 fusion.31
  443.3 5.0 fusion.30
  448.3 1.0 copy.133
  453.1 4.4 all-to-all-start
  459.2 4.8 all-to-all-done
  464.0 4.3 all-to-all-start.1
  469.9 1.0 copy.136
  470.9 4.0 all-to-all-done.1
  475.0 1.0 copy.137
  476.0 44.7 %all-gather.9.cloned.1.call-done = bf16[512,8192]{1,0:T(8,128)(2,1)} async-done(((bf16[128,8192]{1,0:T(8,128)(2,1)}), bf16[512,8192]{1,0:T(8,128)(2,1)}) %all-gather.9.cloned.1.call-update) | async-done | bytes 8388624 | tf_op jit(solution)/shard_map/all_gather | solution.py:16
  520.7 2.5 broadcast_in_dim.42
  523.1 15.9 %while.12 = (s32[]{:T(128)}, f32[128,8192]{1,0:T(8,128)}, s32[]{:T(128)}, bf16[4,128,8192]{2,1,0:T(8,128)(2,1)}, s32[]{:T(128)}, /*index=5*/s32[]{:T(128)}, s32[]{:T(128)}, s32[]{:T(128)}) while((s32[]{:T(128)}, f32[128,8192]{1,0:T(8,128)}, s32[]{:T(128)}, bf16[4,128,8192]{2,1,0:T(8,128)(2,1)}, s32[]{:T(128)}, /*index=5*/s32[]{:T(128)}, ...), condition=%wide.region_15.16_spmd, body=%wide.region_14.15_spmd.sunk | while | flops 2097158 | bytes 10485903 | solution.py:23
  523.1 5.3 convert_add_fusion.2
  528.4 5.3 convert_add_fusion.2
  533.7 5.3 convert_add_fusion.2
  539.0 6.1 %add_bitcast_fusion = f32[1,128,8192]{2,1,0:T(8,128)} fusion(f32[128,8192]{1,0:T(8,128)} %get-tuple-element.62, bf16[128,8192]{1,0:T(8,128)(2,1)} %reduce-scatter.8.cloned.1.call-done, bf16[1,128,8192]{2,1,0:T(8,128)(2,1)S(1)} %copy-done, f32[128]{0:T(128)S(1)} %broadcast_multiply_fusion, f32[128]{0:T(128)S(1)} %get-tuple-element.112, ...), kind=kLoop, calls=%fused_computation.42 | loop fusion | flops 8388608 | bytes 12617216 | tf_op jit(solution)/shard_map/broadcast_in_dim | solution.py:193
  (117 shorter events, 14.1 us)
Async XLA Ops:
  7.2 6.0 %copy-start.25 = (s32[1,2]{1,0:T(1,128)S(1)}, s32[1,2]{1,0:T(1,128)}, u32[]{:S(2)}) copy-start(s32[1,2]{1,0:T(1,128)} %param.24) | copy-start | bytes 28
  7.2 6.0 %copy-start.23 = (s32[1,128]{1,0:T(1,128)S(1)}, s32[1,128]{1,0:T(1,128)}, u32[]{:S(2)}) copy-start(s32[1,128]{1,0:T(1,128)} %param.23) | copy-start | bytes 1540
  7.2 6.1 %copy-start.24 = (s32[3,16]{1,0:T(4,128)S(1)}, s32[3,16]{1,0:T(4,128)}, u32[]{:S(2)}) copy-start(s32[3,16]{1,0:T(4,128)} %param.25) | copy-start | bytes 580
  7.2 6.4 %copy-start.20 = (bf16[1,128,256]{2,1,0:T(8,128)(2,1)S(1)}, bf16[1,128,256]{2,1,0:T(8,128)(2,1)}, u32[]{:S(2)}) copy-start(bf16[1,128,256]{2,1,0:T(8,128)(2,1)} %param.15) | copy-start | bytes 196612
  7.2 6.4 %copy-start.21 = (bf16[1,128,256]{2,1,0:T(8,128)(2,1)S(1)}, bf16[1,128,256]{2,1,0:T(8,128)(2,1)}, u32[]{:S(2)}) copy-start(bf16[1,128,256]{2,1,0:T(8,128)(2,1)} %param.16) | copy-start | bytes 196612
  7.2 72.3 %all-gather.5.cloned.1.call-start = ((), (), s32[]{:S(2)}) async-start(), calls=%async_computation.5 | async-start | bytes 8650752 | tf_op jit(solution)/shard_map/all_gather | solution.py:91
  8.0 138.9 %all-gather.7.cloned.1.call-start = ((), (), s32[]{:S(2)}) async-start(), calls=%async_computation.6 | async-start | bytes 8650752 | tf_op jit(solution)/shard_map/all_gather | solution.py:92
  8.7 280.4 %reduce-scatter.4.cloned.1.call-start = ((), (), s32[]{:S(2)}) async-start(), calls=%async_computation.7 | async-start | bytes 2359296 | tf_op jit(solution)/shard_map/reduce_scatter | solution.py:143
  12.1 137.2 %copy-start.9 = (bf16[1,128,2048]{1,2,0:T(8,128)(2,1)}, bf16[1,128,2048]{1,2,0:T(8,128)(2,1)S(1)}, u32[]{:S(2)}) copy-start(bf16[1,128,2048]{1,2,0:T(8,128)(2,1)S(1)} %copy.108) | copy-start | bytes 1572868
  13.6 137.4 %copy-start.18 = (bf16[128,128]{1,0:T(8,128)(2,1)}, bf16[128,128]{1,0:T(8,128)(2,1)S(1)}, u32[]{:S(2)}) copy-start(bf16[128,128]{1,0:T(8,128)(2,1)S(1)} %get-tuple-element.109) | copy-start | bytes 98308
  149.4 2.6 copy-start.6
  151.0 1.0 copy-start.4
  165.0 11.9 %copy-start.15 = (bf16[4096,128]{1,0:T(8,128)(2,1)S(1)}, bf16[4096,128]{1,0:T(8,128)(2,1)}, u32[]{:S(2)}) copy-start(bf16[4096,128]{1,0:T(8,128)(2,1)} %get-tuple-element.97) | copy-start | bytes 3145732
  165.0 11.9 %copy-start.17 = (bf16[128,1,8,128]{3,0,2,1:T(8,128)(2,1)S(1)}, bf16[128,1,8,128]{3,0,2,1:T(8,128)(2,1)}, u32[]{:S(2)}) copy-start(bf16[128,1,8,128]{3,0,2,1:T(8,128)(2,1)} %copy.162) | copy-start | bytes 786436
  165.0 14.4 %slice-start.5 = ((s8[17301504]{0:T(1024)(128)(4,1)}), s8[4194304]{0:T(1024)(128)(4,1)S(1)}, s32[]{:S(2)}) async-start(s8[17301504]{0:T(1024)(128)(4,1)} %bitcast.163), calls=%async_computation.16 | async-start | bytes 8388608
  165.0 14.4 %slice-start.6 = ((s8[17301504]{0:T(1024)(128)(4,1)}), s8[4194304]{0:T(1024)(128)(4,1)S(1)}, s32[]{:S(2)}) async-start(s8[17301504]{0:T(1024)(128)(4,1)} %bitcast.163), calls=%async_computation.17 | async-start | bytes 8388608
  165.0 14.4 %slice-start.7 = ((s8[17301504]{0:T(1024)(128)(4,1)}), s8[4194304]{0:T(1024)(128)(4,1)S(1)}, s32[]{:S(2)}) async-start(s8[17301504]{0:T(1024)(128)(4,1)} %bitcast.163), calls=%async_computation.18 | async-start | bytes 8388608
  165.0 14.4 %slice-start.8 = ((s8[17301504]{0:T(1024)(128)(4,1)}), s8[4194304]{0:T(1024)(128)(4,1)S(1)}, s32[]{:S(2)}) async-start(s8[17301504]{0:T(1024)(128)(4,1)} %bitcast.163), calls=%async_computation.19 | async-start | bytes 8388608
  172.5 4.4 copy-start.2
  176.9 2.7 slice-start.9
  186.7 7.4 %copy-start.7 = (bf16[1,128,2048]{1,2,0:T(8,128)(2,1)S(1)}, bf16[1,128,2048]{1,2,0:T(8,128)(2,1)}, u32[]{:S(2)}) copy-start(bf16[1,128,2048]{1,2,0:T(8,128)(2,1)} %copy.106) | copy-start | bytes 1572868
  193.1 1.0 copy-start.5
  206.7 11.9 %copy-start.14 = (bf16[4096,128]{1,0:T(8,128)(2,1)S(1)}, bf16[4096,128]{1,0:T(8,128)(2,1)}, u32[]{:S(2)}) copy-start(bf16[4096,128]{1,0:T(8,128)(2,1)} %get-tuple-element.98) | copy-start | bytes 3145732
  206.7 14.4 %slice-start = ((s8[17301504]{0:T(1024)(128)(4,1)}), s8[4194304]{0:T(1024)(128)(4,1)S(1)}, s32[]{:S(2)}) async-start(s8[17301504]{0:T(1024)(128)(4,1)} %bitcast.161), calls=%async_computation.11 | async-start | bytes 8388608
  206.7 14.4 %slice-start.1 = ((s8[17301504]{0:T(1024)(128)(4,1)}), s8[4194304]{0:T(1024)(128)(4,1)S(1)}, s32[]{:S(2)}) async-start(s8[17301504]{0:T(1024)(128)(4,1)} %bitcast.161), calls=%async_computation.12 | async-start | bytes 8388608
  206.7 14.4 %slice-start.2 = ((s8[17301504]{0:T(1024)(128)(4,1)}), s8[4194304]{0:T(1024)(128)(4,1)S(1)}, s32[]{:S(2)}) async-start(s8[17301504]{0:T(1024)(128)(4,1)} %bitcast.161), calls=%async_computation.13 | async-start | bytes 8388608
  206.7 14.4 %slice-start.3 = ((s8[17301504]{0:T(1024)(128)(4,1)}), s8[4194304]{0:T(1024)(128)(4,1)S(1)}, s32[]{:S(2)}) async-start(s8[17301504]{0:T(1024)(128)(4,1)} %bitcast.161), calls=%async_computation.14 | async-start | bytes 8388608
  214.2 4.4 copy-start.3
  218.6 2.6 slice-start.4
  221.2 7.2 %copy-start.8 = (bf16[1,128,2048]{1,2,0:T(8,128)(2,1)S(1)}, bf16[1,128,2048]{1,2,0:T(8,128)(2,1)}, u32[]{:S(2)}) copy-start(bf16[1,128,2048]{1,2,0:T(8,128)(2,1)} %copy.106) | copy-start | bytes 1572868
  228.4 7.5 %slice-start.10 = ((bf16[4224,128]{0,1:T(8,128)(2,1)}), bf16[4096,128]{0,1:T(8,128)(2,1)S(1)}, s32[]{:S(2)}) async-start(bf16[4224,128]{0,1:T(8,128)(2,1)} %copy-done.5), calls=%async_computation.21 | async-start | bytes 2097152 | tf_op jit(solution)/shard_map/slice | solution.py:133
  234.9 1.0 copy-start.11
  235.9 1.7 copy-start.10
  237.5 105.6 %reduce-scatter.6.cloned.1.call-start = ((), (), s32[]{:S(2)}) async-start(), calls=%async_computation.8 | async-start | bytes 2359296 | tf_op jit(solution)/shard_map/reduce_scatter | solution.py:146
  244.0 1.0 copy-start.13
  251.5 1.7 copy-start.12
  253.2 179.1 %reduce-scatter.8.cloned.1.call-start = ((), (), s32[]{:S(2)}) async-start(), calls=%async_computation.9 | async-start | bytes 10485760 | tf_op jit(solution)/shard_map/reduce_scatter | solution.py:170
  354.6 0.8 copy-start.22
  354.6 77.7 %copy-start = (bf16[1,128,8192]{2,1,0:T(8,128)(2,1)S(1)}, bf16[1,128,8192]{2,1,0:T(8,128)(2,1)}, u32[]{:S(2)}) copy-start(bf16[1,128,8192]{2,1,0:T(8,128)(2,1)} %param.21) | copy-start | bytes 6291460
  354.7 166.0 %all-gather.9.cloned.1.call-start = ((), (), s32[]{:S(2)}) async-start(), calls=%async_computation.10 | async-start | bytes 10485760 | tf_op jit(solution)/shard_map/all_gather | solution.py:16
  432.4 2.8 copy-start.1
  435.2 2.9 copy-start.19
  443.2 9.1 %copy-start.16 = (bf16[512,256]{0,1:T(8,128)(2,1)S(1)}, bf16[512,256]{0,1:T(8,128)(2,1)}, u32[]{:S(2)}) copy-start(bf16[512,256]{0,1:T(8,128)(2,1)} %reduce-scatter.4.cloned.1.call-done) | copy-start | bytes 786436
  453.1 10.9 %all-to-all-start = ((bf16[4,128,256]{1,2,0:T(8,128)(2,1)}), bf16[4,128,256]{1,2,0:T(8,128)(2,1)S(1)}, u32[]{:S(2)}, u32[]{:S(2)}) async-start(bf16[4,128,256]{1,2,0:T(8,128)(2,1)} %copy_bitcast_fusion), calls=%async_computation.1 | async-start | bytes 524288 | tf_op jit(solution)/shard_map/all_to_all | solution.py:151
  464.0 10.9 %all-to-all-start.1 = ((bf16[4,128,256]{1,2,0:T(8,128)(2,1)}), bf16[4,128,256]{1,2,0:T(8,128)(2,1)S(1)}, u32[]{:S(2)}, u32[]{:S(2)}) async-start(bf16[4,128,256]{1,2,0:T(8,128)(2,1)} %pad_maximum_fusion.3), calls=%async_computation.3 | async-start | bytes 524288 | tf_op jit(solution)/shard_map/all_to_all | solution.py:155
Sparse Core Ops, SparseCore 0:
  9.7 69.7 all-gather.4
  81.3 65.5 all-gather.6
  237.7 51.3 reduce-scatter.3
  291.3 51.8 reduce-scatter.5
  354.8 77.5 reduce-scatter.7
  438.2 82.4 all-gather.8
